TPU v7x, 32 devices: a whole 2x2x4 slice. The times are simulated.
32 devices in a mesh: grp: 4 (over z), seq: 8 (over y, x, core).
Axes of the slice: x: 2, y: 2, z: 4, core: 2. Of those that a mesh axis runs over, the one named last changes fastest.
Arguments:
- queries: bfloat16 [32768, 1024], P(('grp', 'seq')), may hold values from -6 to 6
- keys: bfloat16 [32768, 1024], P(('grp', 'seq')), may hold values from -6 to 6
- values: bfloat16 [32768, 1024], P(('grp', 'seq')), may hold values from -4 to 4
- cache_kv: bfloat16 [2, 128, 1024, 512], P(None, 'grp', 'seq'), may hold values from -4 to 4
- thread_start: int32 [32], replicated, may hold values from 1024 to 162816, as said below
Outputs:
- attended: bfloat16 [32768, 1024], P(('grp', 'seq'))
Inputs may be any that keep to these rules, and one draw needn't show every extreme that they name: `thread_start`: Non-decreasing multiples of 1024; rows with equal entries are consecutive and form one thread. The first window rows belong to a thread that began inside the cache: their entry is s * 1024 for a cached context row s with 1 <= s <= 64. Every later thread begins at a window row b > 0, and its entry is (128 + b) * 1024; the last row begins a thread of its own.
All inputs are finite; a program needn't handle non-finite values.
Results may differ from a plain program's by a relative error of at most 0.0028.
Values may be sent and summed in bfloat16 or wider, within the bound.
No kernel may reach another device: no remote copies, remote signals or barrier semaphores. Data moves between devices by JAX's collectives and lax.ppermute only.
A program may use at most 256 MiB of HBM per device.

v0:
```python
import jax
import jax.numpy as jnp
from jax import lax
from jax.sharding import PartitionSpec as P

LH = 8
SH = 8
HD = 64
STRIDE = 1024
CACHE = 128


def local_attention(q_part, k_part, v_part):
    scale = HD ** (-0.5)
    tok = q_part.shape[0]
    rows_dev = tok // STRIDE
    block = min(512, STRIDE)
    per_row = STRIDE // block
    q_blocks = q_part.reshape(tok // block, block, LH, HD)
    k_rows = k_part.reshape(rows_dev, STRIDE, LH, HD)
    v_rows = v_part.reshape(rows_dev, STRIDE, LH, HD)
    key_place = jnp.arange(STRIDE, dtype=jnp.int32)

    def one_block(index):
        row_index = index // per_row
        first = index % per_row * block
        query = lax.dynamic_index_in_dim(q_blocks, index, 0, keepdims=False)
        key_row = lax.dynamic_index_in_dim(k_rows, row_index, 0, keepdims=False)
        value_row = lax.dynamic_index_in_dim(v_rows, row_index, 0, keepdims=False)
        scores = (
            jnp.einsum("qhd,khd->hqk", query, key_row, preferred_element_type=jnp.float32) * scale
        )
        causal = (first + jnp.arange(block, dtype=jnp.int32))[:, None] >= key_place[None, :]
        scores = jnp.where(causal[None], scores, -jnp.inf)
        top = jnp.max(scores, axis=-1, keepdims=True)
        expo = jnp.exp(scores - top)
        total = jnp.sum(expo, axis=-1)
        mixed = jnp.einsum(
            "hqk,khd->qhd", expo.astype(jnp.bfloat16), value_row, preferred_element_type=jnp.float32
        )
        return (mixed / jnp.transpose(total)[:, :, None]).reshape(block, LH * HD)

    result = lax.map(one_block, jnp.arange(tok // block, dtype=jnp.int32))
    return result.reshape(tok, LH * HD)


def fresh_state(query_stack):
    rows_here = query_stack.shape[1]
    cols_here = query_stack.shape[2]
    top = jnp.full((cols_here, SH, rows_here), -1e30, jnp.float32)
    total = jnp.zeros((cols_here, SH, rows_here), jnp.float32)
    acc = jnp.zeros((cols_here, SH, rows_here, HD), jnp.float32)
    return (top, total, acc)


def absorb(state, query, piece, key_rows, query_rows, starts):
    scale = HD ** (-0.5)
    top, total, acc = state
    rows_here = query.shape[0]
    cols_here = query.shape[1]
    count = piece.shape[1]
    q_heads = query.reshape(rows_here, cols_here, SH, HD)
    k_heads = piece[0].reshape(count, cols_here, SH, HD)
    v_heads = piece[1].reshape(count, cols_here, SH, HD)
    scores = (
        jnp.einsum("rchd,mchd->chrm", q_heads, k_heads, preferred_element_type=jnp.float32) * scale
    )
    visible = (key_rows[None, :] >= starts[:, None]) & (
        key_rows[None, :] <= CACHE + query_rows[:, None]
    )
    scores = jnp.where(visible, scores, -1e30)
    new_top = jnp.maximum(top, jnp.max(scores, axis=-1))
    weights = jnp.where(visible, jnp.exp(scores - new_top[..., None]), 0.0)
    keep = jnp.exp(top - new_top)
    total = jnp.sum(weights, axis=-1)
    acc = jnp.einsum(
        "chrm,mchd->chrd", weights.astype(jnp.bfloat16), v_heads, preferred_element_type=jnp.float32
    )
    return (new_top, total, acc)


def finish_state(state):
    top, total, acc = state
    mixed = acc / total[..., None]
    cols_here, heads, rows_here, depth = mixed.shape
    return (
        jnp.transpose(mixed, (2, 0, 1, 3))
        .reshape(rows_here, cols_here, heads * depth)
        .astype(jnp.bfloat16)
    )


def shards(queries, keys, values, cache_kv, thread_start):
    width_l = LH * HD
    width_s = SH * HD
    tok = queries.shape[0]
    rows_dev = tok // STRIDE
    strided_q = queries[:, width_l:].reshape(1, rows_dev, STRIDE, width_s)
    strided_kv = jnp.stack([keys[:, width_l:], values[:, width_l:]]).reshape(
        2, rows_dev, STRIDE, width_s
    )
    group_q, group_kv = (
        lax.all_to_all(strided_q, "seq", split_axis=2, concat_axis=1, tiled=True),
        lax.all_to_all(strided_kv, "seq", split_axis=2, concat_axis=1, tiled=True),
    )
    local_out = local_attention(queries[:, :width_l], keys[:, :width_l], values[:, :width_l])
    starts_all = thread_start // STRIDE
    rows_all = thread_start.shape[0]
    all_q, all_kv, cached = (
        lax.all_to_all(group_q, "grp", split_axis=2, concat_axis=1, tiled=True),
        lax.all_to_all(group_kv, "grp", split_axis=2, concat_axis=1, tiled=True),
        lax.all_to_all(cache_kv, "grp", split_axis=2, concat_axis=1, tiled=True),
    )
    pieces = jnp.concatenate([cached, all_kv], axis=1)
    key_rows = jnp.arange(CACHE + rows_all, dtype=jnp.int32)
    query_rows = jnp.arange(rows_all, dtype=jnp.int32)
    state = absorb(fresh_state(all_q), all_q[0], pieces, key_rows, query_rows, starts_all)
    result = lax.all_to_all(finish_state(state), "grp", split_axis=0, concat_axis=1, tiled=True)
    back = lax.all_to_all(result, "seq", split_axis=0, concat_axis=1, tiled=True)
    strided_out = back.reshape(tok, width_s)
    return jnp.concatenate([local_out.astype(jnp.bfloat16), strided_out], axis=1)


def solution(mesh):
    placed = (
        P(("grp", "seq"), None),
        P(("grp", "seq"), None),
        P(("grp", "seq"), None),
        P(None, "grp", "seq", None),
        P(),
    )
    return jax.shard_map(
        shards, mesh=mesh, in_specs=placed, out_specs=P(("grp", "seq"), None), check_vma=False
    )
```

profile of v0, /device:TPU:0, one launch (start us, length us, event | category | flops | bytes accessed | tf_op | source)
XLA Modules:
  0.0 477.3 jit_solution(8465424382512381925)
XLA Ops:
  4.8 7.0 %reduce = bf16[1024,512]{1,0:T(8,128)(2,1)S(1)} reduce(bf16[1024,1,1,512]{3,2,1,0:T(2,128)(2,1)S(1)} %bitcast.102, bf16[]{:T(256)} %broadcast.73), dimensions={1,2}, to_apply=%bitcast.80.reduce_sub_computation | reduce | bytes 2097154
  13.4 5.4 %all-to-all-start.3 = ((bf16[8,2,32768]{2,1,0:T(2,128)(2,1)}), bf16[8,2,32768]{2,1,0:T(2,128)(2,1)S(1)}, u32[]{:S(2)}, u32[]{:S(2)}) async-start(bf16[8,2,32768]{2,1,0:T(2,128)(2,1)} %reshape.87), calls=%async_computation.3 | async-start | bytes 2097152 | tf_op jit(solution)/shard_map/all_to_all | solution.py:103
  18.9 3.9 fusion.44
  22.9 3.5 copy.60
  26.4 7.8 %all-to-all-done.3 = bf16[8,2,32768]{2,1,0:T(2,128)(2,1)S(1)} async-done(((bf16[8,2,32768]{2,1,0:T(2,128)(2,1)}), bf16[8,2,32768]{2,1,0:T(2,128)(2,1)S(1)}, u32[]{:S(2)}, u32[]{:S(2)}) %all-to-all-start.3) | async-done | bytes 1048608 | tf_op jit(solution)/shard_map/all_to_all | solution.py:103
  34.2 4.4 all-to-all-start.1
  41.5 23.7 %all-to-all-done.1 = bf16[2,1,1024,512]{3,0,1,2:T(2,128)(2,1)} async-done(((bf16[2,1,1024,512]{3,0,1,2:T(2,128)(2,1)}), bf16[2,1,1024,512]{3,0,1,2:T(2,128)(2,1)}, u32[]{:S(2)}, u32[]{:S(2)}) %all-to-all-start.1) | async-done | bytes 2097184 | tf_op jit(solution)/shard_map/all_to_all | solution.py:104
  65.2 4.9 %all-to-all-start.4 = ((bf16[1,8,128,512]{3,1,0,2:T(8,128)(2,1)}), bf16[1,8,128,512]{3,1,0,2:T(8,128)(2,1)S(1)}, u32[]{:S(2)}, u32[]{:S(2)}) async-start(bf16[1,8,128,512]{3,1,0,2:T(8,128)(2,1)} %copy.66), calls=%async_computation.4 | async-start | bytes 2097152 | tf_op jit(solution)/shard_map/all_to_all | solution.py:110
  70.0 5.1 %copy.61 = bf16[2,8,128,512]{3,1,0,2:T(8,128)(2,1)} copy(bf16[2,8,128,512]{3,0,2,1:T(2,128)(2,1)} %bitcast.10) | data formatting | bytes 4194304 | tf_op jit(solution)/shard_map/all_to_all | solution.py:104
  75.2 17.6 %all-to-all-done.4 = bf16[1,8,128,512]{3,1,0,2:T(8,128)(2,1)S(1)} async-done(((bf16[1,8,128,512]{3,1,0,2:T(8,128)(2,1)}), bf16[1,8,128,512]{3,1,0,2:T(8,128)(2,1)S(1)}, u32[]{:S(2)}, u32[]{:S(2)}) %all-to-all-start.4) | async-done | bytes 1048608 | tf_op jit(solution)/shard_map/all_to_all | solution.py:110
  92.8 3.6 all-to-all-start.2
  96.5 11.3 %copy.57 = bf16[2,32,128,512]{3,1,0,2:T(8,128)(2,1)} copy(bf16[2,32,128,512]{3,2,1,0:T(8,128)(2,1)} %param.10) | data formatting | bytes 16777216 | tf_op args[3]
  107.8 35.8 %all-to-all-done.2 = bf16[2,8,128,512]{3,1,0,2:T(8,128)(2,1)S(1)} async-done(((bf16[2,8,128,512]{3,1,0,2:T(8,128)(2,1)}), bf16[2,8,128,512]{3,1,0,2:T(8,128)(2,1)S(1)}, u32[]{:S(2)}, u32[]{:S(2)}) %all-to-all-start.2) | async-done | bytes 2097184 | tf_op jit(solution)/shard_map/all_to_all | solution.py:111
  143.6 5.9 %all-to-all-start = ((bf16[2,32,128,512]{3,1,0,2:T(8,128)(2,1)}), bf16[2,32,128,512]{3,1,0,2:T(8,128)(2,1)}, u32[]{:S(2)}, u32[]{:S(2)}) async-start(bf16[2,32,128,512]{3,1,0,2:T(8,128)(2,1)} %copy.57), calls=%async_computation | async-start | bytes 16777216 | tf_op jit(solution)/shard_map/all_to_all | solution.py:112
  151.2 4.1 copy.63
  155.3 176.9 %all-to-all-done = bf16[2,32,128,512]{3,1,0,2:T(8,128)(2,1)} async-done(((bf16[2,32,128,512]{3,1,0,2:T(8,128)(2,1)}), bf16[2,32,128,512]{3,1,0,2:T(8,128)(2,1)}, u32[]{:S(2)}, u32[]{:S(2)}) %all-to-all-start) | async-done | bytes 8388640 | tf_op jit(solution)/shard_map/all_to_all | solution.py:112
  332.2 12.0 %copy.59 = bf16[2,4,32,32,512]{4,3,2,1,0:T(8,128)(2,1)} copy(bf16[2,4,32,32,512]{4,2,0,3,1:T(8,128)(2,1)} %bitcast.5) | data formatting | bytes 16777216 | tf_op jit(solution)/shard_map/all_to_all | solution.py:112
  344.2 7.8 %pad_maximum_fusion = (bf16[1,160,32,512]{3,2,1,0:T(8,128)(2,1)}, bf16[1,160,32,512]{3,2,1,0:T(8,128)(2,1)}) fusion(bf16[2,32,32,512]{3,2,1,0:T(8,128)(2,1)S(1)} %bitcast.99, bf16[2,128,32,512]{3,2,1,0:T(8,128)(2,1)} %bitcast.96), kind=kLoop, calls=%fused_computation.29 | loop fusion | flops 5242880 | bytes 20971520 | tf_op jit(solution)/shard_map/concatenate | solution.py:114
  352.0 12.8 %copy.64 = bf16[1,160,32,512]{1,3,2,0:T(8,128)(2,1)} copy(bf16[1,160,32,512]{3,2,1,0:T(8,128)(2,1)} %get-tuple-element.149) | data formatting | bytes 10485760 | tf_op jit(solution)/shard_map/slice | solution.py:63
  364.7 9.1 %fusion.24 = (f32[32,8,32]{2,1,0:T(8,128)S(1)}, f32[32,8,160,32]{2,3,1,0:T(8,128)}) fusion(pred[32,160]{1,0:T(8,128)(4,1)S(1)} %fusion.40, bf16[160,32,8,64]{0,3,2,1:T(8,128)(2,1)} %bitcast.97, bf16[32,32,8,64]{3,2,1,0:T(8,128)(2,1)S(1)} %reshape_squeeze.10), kind=kOutput, calls=%fused_computation.25 | convolution fusion | flops 171696128 | bytes 11572224 | tf_op jit(solution)/shard_map/rchd,mchd->chrm/dot_general | solution.py:66
  373.8 12.8 %copy.70 = bf16[1,160,32,512]{1,3,2,0:T(8,128)(2,1)} copy(bf16[1,160,32,512]{3,2,1,0:T(8,128)(2,1)} %get-tuple-element.148) | data formatting | bytes 10485760 | tf_op jit(solution)/shard_map/slice | solution.py:64
  386.6 5.4 %fusion.25 = f32[32,8,32]{2,1,0:T(8,128)S(1)} fusion(f32[32,8,160,32]{2,3,1,0:T(8,128)} %get-tuple-element.157, f32[32,8,32]{2,1,0:T(8,128)S(1)} %broadcast_maximum_fusion, pred[32,160]{1,0:T(8,128)(4,1)S(1)} %fusion.40), kind=kLoop, calls=%fused_computation.26 | loop fusion | flops 6545408 | bytes 5313536 | tf_op jit(solution)/shard_map/reduce_sum | solution.py:75
  392.4 6.0 %fusion.30 = bf16[32,32,8,64]{3,0,2,1:T(8,128)(2,1)S(1)} fusion(f32[32,32,8]{0,2,1:T(8,128)S(1)} %bitcast.110, bf16[160,32,8,64]{0,3,2,1:T(8,128)(2,1)S(1)} %bitcast.103, f32[32,8,160,32]{2,3,1,0:T(8,128)} %get-tuple-element.157, f32[32,8,32]{2,1,0:T(8,128)S(1)} %broadcast_maximum_fusion, pred[32,160]{1,0:T(8,128)(4,1)S(1)} %fusion.40), kind=kOutput, calls=%fused_computation.32 | convolution fusion | flops 175374336 | bytes 11604992 | tf_op jit(solution)/shard_map/chrm,mchd->chrd/dot_general | solution.py:76
  401.3 4.3 all-to-all-start.5
  414.0 17.0 %all-to-all-done.5 = bf16[32,32,512]{2,1,0:T(8,128)(2,1)} async-done(((bf16[32,32,512]{2,1,0:T(8,128)(2,1)}), bf16[32,32,512]{2,1,0:T(8,128)(2,1)}, u32[]{:S(2)}, u32[]{:S(2)}) %all-to-all-start.5) | async-done | bytes 1048608 | tf_op jit(solution)/shard_map/all_to_all | solution.py:118
  433.3 5.5 %all-to-all-start.6 = ((bf16[8,128,512]{2,1,0:T(8,128)(2,1)}), bf16[8,128,512]{2,1,0:T(8,128)(2,1)}, u32[]{:S(2)}, u32[]{:S(2)}) async-start(bf16[8,128,512]{2,1,0:T(8,128)(2,1)} %bitcast.105), calls=%async_computation.6 | async-start | bytes 2097152 | tf_op jit(solution)/shard_map/all_to_all | solution.py:119
  438.8 33.8 %while.13 = (s32[]{:T(128)}, bf16[2,512,512]{1,2,0:T(8,128)(2,1)}, s32[2]{0:T(128)S(1)}, bf16[2,512,8,64]{1,3,2,0:T(8,128)(2,1)S(1)}, bf16[1,1024,8,64]{1,3,2,0:...) while((s32[]{:T(128)}, bf16[2,512,512]{1,2,0:T(8,128)(2,1)}, ...), condition=%wide.region_3.4_spmd.clone, body=%wide.region_0.3_spmd.clone.sunk | while | flops 1120920064 | bytes 60904232 | solution.py:43
  443.0 2.9 fusion.56
  445.9 4.2 fusion.57
  450.1 4.7 fusion.58
  462.7 4.2 fusion.57
  467.0 4.7 fusion.58
  (49 shorter events, 35.9 us)
Async XLA Ops:
  13.4 20.7 %all-to-all-start.3 = ((bf16[8,2,32768]{2,1,0:T(2,128)(2,1)}), bf16[8,2,32768]{2,1,0:T(2,128)(2,1)S(1)}, u32[]{:S(2)}, u32[]{:S(2)}) async-start(bf16[8,2,32768]{2,1,0:T(2,128)(2,1)} %reshape.87), calls=%async_computation.3 | async-start | bytes 2097152 | tf_op jit(solution)/shard_map/all_to_all | solution.py:103
  34.2 31.0 %all-to-all-start.1 = ((bf16[2,1,1024,512]{3,0,1,2:T(2,128)(2,1)}), bf16[2,1,1024,512]{3,0,1,2:T(2,128)(2,1)}, u32[]{:S(2)}, u32[]{:S(2)}) async-start(bf16[2,1,1024,512]{3,0,1,2:T(2,128)(2,1)} %copy.60), calls=%async_computation.1 | async-start | bytes 4194304 | tf_op jit(solution)/shard_map/all_to_all | solution.py:104
  65.2 27.7 %all-to-all-start.4 = ((bf16[1,8,128,512]{3,1,0,2:T(8,128)(2,1)}), bf16[1,8,128,512]{3,1,0,2:T(8,128)(2,1)S(1)}, u32[]{:S(2)}, u32[]{:S(2)}) async-start(bf16[1,8,128,512]{3,1,0,2:T(8,128)(2,1)} %copy.66), calls=%async_computation.4 | async-start | bytes 2097152 | tf_op jit(solution)/shard_map/all_to_all | solution.py:110
  92.8 50.8 %all-to-all-start.2 = ((bf16[2,8,128,512]{3,1,0,2:T(8,128)(2,1)}), bf16[2,8,128,512]{3,1,0,2:T(8,128)(2,1)S(1)}, u32[]{:S(2)}, u32[]{:S(2)}) async-start(bf16[2,8,128,512]{3,1,0,2:T(8,128)(2,1)} %copy.61), calls=%async_computation.2 | async-start | bytes 4194304 | tf_op jit(solution)/shard_map/all_to_all | solution.py:111
  107.8 41.7 %copy-start.5 = (s32[32]{0:T(128)S(1)}, s32[32]{0:T(128)}, u32[]{:S(2)}) copy-start(s32[32]{0:T(128)} %param.11) | copy-start | bytes 388
  143.6 5.9 %copy-start.1 = (bf16[2,8,128,512]{3,1,0,2:T(8,128)(2,1)}, bf16[2,8,128,512]{3,1,0,2:T(8,128)(2,1)S(1)}, u32[]{:S(2)}) copy-start(bf16[2,8,128,512]{3,1,0,2:T(8,128)(2,1)S(1)} %all-to-all-done.2) | copy-start | bytes 6291460
  143.6 188.5 %all-to-all-start = ((bf16[2,32,128,512]{3,1,0,2:T(8,128)(2,1)}), bf16[2,32,128,512]{3,1,0,2:T(8,128)(2,1)}, u32[]{:S(2)}, u32[]{:S(2)}) async-start(bf16[2,32,128,512]{3,1,0,2:T(8,128)(2,1)} %copy.57), calls=%async_computation | async-start | bytes 16777216 | tf_op jit(solution)/shard_map/all_to_all | solution.py:112
  332.2 12.0 %copy-start = (bf16[2,4,8,32,512]{4,3,2,1,0:T(8,128)(2,1)S(1)}, bf16[2,4,8,32,512]{4,3,2,1,0:T(8,128)(2,1)}, u32[]{:S(2)}) copy-start(bf16[2,4,8,32,512]{4,3,2,1,0:T(8,128)(2,1)} %copy.63) | copy-start | bytes 6291460
  386.6 5.8 %copy-start.2 = (bf16[1,160,32,512]{1,3,2,0:T(8,128)(2,1)S(1)}, bf16[1,160,32,512]{1,3,2,0:T(8,128)(2,1)}, u32[]{:S(2)}) copy-start(bf16[1,160,32,512]{1,3,2,0:T(8,128)(2,1)} %copy.70) | copy-start | bytes 15728644
  398.5 10.9 %copy-start.3 = (bf16[1024,512]{1,0:T(8,128)(2,1)S(1)}, bf16[1024,512]{1,0:T(8,128)(2,1)}, u32[]{:S(2)}) copy-start(bf16[1024,512]{1,0:T(8,128)(2,1)} %get-tuple-element.154) | copy-start | bytes 3145732
  401.3 29.6 %all-to-all-start.5 = ((bf16[32,32,512]{2,1,0:T(8,128)(2,1)}), bf16[32,32,512]{2,1,0:T(8,128)(2,1)}, u32[]{:S(2)}, u32[]{:S(2)}) async-start(bf16[32,32,512]{2,1,0:T(8,128)(2,1)} %convert_element_type.25), calls=%async_computation.5 | async-start | bytes 2097152 | tf_op jit(solution)/shard_map/all_to_all | solution.py:118
  433.3 40.8 %all-to-all-start.6 = ((bf16[8,128,512]{2,1,0:T(8,128)(2,1)}), bf16[8,128,512]{2,1,0:T(8,128)(2,1)}, u32[]{:S(2)}, u32[]{:S(2)}) async-start(bf16[8,128,512]{2,1,0:T(8,128)(2,1)} %bitcast.105), calls=%async_computation.6 | async-start | bytes 2097152 | tf_op jit(solution)/shard_map/all_to_all | solution.py:119
  445.9 4.2 copy-start.4
  462.7 4.2 copy-start.4
where the time goes:
time: 486 us; the launch traced here: 477 us
  waiting for transfers between devices  279 us (57%)
  local copies, waits for them, and re-layouts  94.6 us (19%)
  starting transfers between devices  33.9 us (7%)
  other arithmetic  32.5 us (7%)
  matrix products  30.3 us (6%)
  loops' own time  6.48 us (1%)
    all_to_all x1, waiting for transfers between devices, shards(): lax.all_to_all(cache_kv, 'grp', split_axis=2, concat_axis=1, tiled=True)  177 us
    all_to_all x1, waiting for transfers between devices, shards(): lax.all_to_all(group_kv, 'grp', split_axis=2, concat_axis=1, tiled=True)  35.8 us
    all_to_all x1, waiting for transfers between devices, shards(): lax.all_to_all(strided_kv, 'seq', split_axis=2, concat_axis=1, tiled=True)  23.7 us
    unnamed x16, local copies, waits for them, and re-layouts  17.8 us
    all_to_all x1, waiting for transfers between devices, shards(): lax.all_to_all(group_q, 'grp', split_axis=2, concat_axis=1, tiled=True)  17.6 us
    all_to_all x1, waiting for transfers between devices, shards(): lax.all_to_all(finish_state(state), 'grp', split_axis=0, concat_axis=1, t...  17 us
    slice x1, local copies, waits for them, and re-layouts, absorb(): v_heads = piece[1].reshape(count, cols_here, SH, HD)  12.8 us
    slice x1, local copies, waits for them, and re-layouts, absorb(): k_heads = piece[0].reshape(count, cols_here, SH, HD)  12.8 us
  transfers between devices with their start and end apart: 7, of which 6 were waited for; matrix products, arithmetic and copies ran while one was open for 15% of the time, Pallas kernels for 0%

commit v1 on v0

v1 whole, which is shorter than its diff:
```python
import jax
import jax.numpy as jnp
from jax import lax
from jax.sharding import PartitionSpec as P

LH = 8
SH = 8
HD = 64
STRIDE = 1024
CACHE = 128


def local_attention(q_part, k_part, v_part):
    scale = HD ** (-0.5)
    tok = q_part.shape[0]
    rows_dev = tok // STRIDE
    block = min(512, STRIDE)
    per_row = STRIDE // block
    q_blocks = q_part.reshape(tok // block, block, LH, HD)
    k_rows = k_part.reshape(rows_dev, STRIDE, LH, HD)
    v_rows = v_part.reshape(rows_dev, STRIDE, LH, HD)
    key_place = jnp.arange(STRIDE, dtype=jnp.int32)

    def one_block(index):
        row_index = index // per_row
        first = index % per_row * block
        query = lax.dynamic_index_in_dim(q_blocks, index, 0, keepdims=False)
        key_row = lax.dynamic_index_in_dim(k_rows, row_index, 0, keepdims=False)
        value_row = lax.dynamic_index_in_dim(v_rows, row_index, 0, keepdims=False)
        scores = (
            jnp.einsum("qhd,khd->hqk", query, key_row, preferred_element_type=jnp.float32) * scale
        )
        causal = (first + jnp.arange(block, dtype=jnp.int32))[:, None] >= key_place[None, :]
        scores = jnp.where(causal[None], scores, -jnp.inf)
        top = jnp.max(scores, axis=-1, keepdims=True)
        expo = jnp.exp(scores - top)
        total = jnp.sum(expo, axis=-1)
        mixed = jnp.einsum(
            "hqk,khd->qhd", expo.astype(jnp.bfloat16), value_row, preferred_element_type=jnp.float32
        )
        return (mixed / jnp.transpose(total)[:, :, None]).reshape(block, LH * HD)

    result = lax.map(one_block, jnp.arange(tok // block, dtype=jnp.int32))
    return result.reshape(tok, LH * HD)


def strided_attention(queries, keys, values, cache_kv, thread_start):
    scale = HD ** (-0.5)
    width_l = LH * HD
    width_s = SH * HD
    tok = queries.shape[0]
    rows_dev = tok // STRIDE
    cache_here = cache_kv.shape[1]
    cols_here = cache_kv.shape[2]
    rows_all = thread_start.shape[0]
    grp = lax.axis_index("grp")

    own_q = queries[:, width_l:].reshape(rows_dev, STRIDE, width_s)
    own_kv = jnp.stack([keys[:, width_l:], values[:, width_l:]]).reshape(2, rows_dev, STRIDE, width_s)
    plane_q = lax.all_to_all(own_q, "seq", split_axis=1, concat_axis=0, tiled=True)
    plane_kv = lax.all_to_all(own_kv, "seq", split_axis=2, concat_axis=1, tiled=True)
    rows_plane = plane_q.shape[0]
    all_q = lax.all_gather(plane_q, "grp", axis=0, tiled=True)

    k_here = jnp.concatenate([cache_kv[0], plane_kv[0]], axis=0)
    v_here = jnp.concatenate([cache_kv[1], plane_kv[1]], axis=0)
    count = k_here.shape[0]
    key_rows = jnp.concatenate(
        [
            grp * cache_here + jnp.arange(cache_here, dtype=jnp.int32),
            CACHE + grp * rows_plane + jnp.arange(rows_plane, dtype=jnp.int32),
        ]
    )
    starts = thread_start // STRIDE
    query_rows = jnp.arange(rows_all, dtype=jnp.int32)
    visible = (key_rows[None, :] >= starts[:, None]) & (key_rows[None, :] <= CACHE + query_rows[:, None])

    q_heads = all_q.reshape(rows_all, cols_here, SH, HD)
    k_heads = k_here.reshape(count, cols_here, SH, HD)
    v_heads = v_here.reshape(count, cols_here, SH, HD)
    scores = (
        jnp.einsum("rchd,mchd->chrm", q_heads, k_heads, preferred_element_type=jnp.float32) * scale
    )
    scores = jnp.where(visible, scores, -jnp.inf)
    top = lax.pmax(jnp.max(scores, axis=-1), "grp")
    expo = jnp.exp(scores - top[..., None])
    total = jnp.sum(expo, axis=-1)
    acc = jnp.einsum(
        "chrm,mchd->rchd", expo.astype(jnp.bfloat16), v_heads, preferred_element_type=jnp.float32
    )
    packed = jnp.concatenate(
        [
            acc.reshape(rows_all, cols_here * width_s),
            jnp.transpose(total, (2, 0, 1)).reshape(rows_all, cols_here * SH),
        ],
        axis=1,
    )
    summed = lax.psum_scatter(packed, "grp", scatter_dimension=0, tiled=True)
    acc_mine = summed[:, : cols_here * width_s].reshape(rows_plane, cols_here, SH, HD)
    total_mine = summed[:, cols_here * width_s :].reshape(rows_plane, cols_here, SH)
    mixed = (acc_mine / total_mine[..., None]).astype(jnp.bfloat16)
    mixed = mixed.reshape(rows_plane, cols_here, width_s)
    back = lax.all_to_all(mixed, "seq", split_axis=0, concat_axis=1, tiled=True)
    return back.reshape(tok, width_s)


def shards(queries, keys, values, cache_kv, thread_start):
    width_l = LH * HD
    strided_out = strided_attention(queries, keys, values, cache_kv, thread_start)
    local_out = local_attention(queries[:, :width_l], keys[:, :width_l], values[:, :width_l])
    return jnp.concatenate([local_out.astype(jnp.bfloat16), strided_out], axis=1)


def solution(mesh):
    placed = (
        P(("grp", "seq"), None),
        P(("grp", "seq"), None),
        P(("grp", "seq"), None),
        P(None, "grp", "seq", None),
        P(),
    )
    return jax.shard_map(
        shards, mesh=mesh, in_specs=placed, out_specs=P(("grp", "seq"), None), check_vma=False
    )
```

time: 486 us -> 467 us (0.961)
  waiting for transfers between devices: 279 us -> 174 us
  local copies, waits for them, and re-layouts: 94.6 us -> 156 us
  starting transfers between devices: 33.9 us -> 7.36 us
  blocking collectives: 0 us -> 20.8 us
  between operations: 0.65 us -> 13.5 us
  matrix products: 30.3 us -> 40.9 us
  other arithmetic: 32.5 us -> 39.5 us
    all_to_all x7 -> x2, waiting for transfers between devices: 279 us -> 0.82 us  [the longest x1 0.82 us: strided_attention(): lax.all_to_all(own_kv, 'seq', split_axis=2, concat_axis=1, tiled=True)]
    reduce_scatter x0 -> x1, waiting for transfers between devices: none -> 138 us  [strided_attention(): summed = lax.psum_scatter(packed, 'grp', scatter_dimension=0, tiled=True)]
    concatenate x0 -> x6, local copies, waits for them, and re-layouts: none -> 38.8 us  [the longest x3 19.6 us: strided_attention(): k_here = jnp.concatenate([cache_kv[0], plane_kv[0]], axis=0)]
    reshape x2 -> x6, local copies, waits for them, and re-layouts: 5.09 us -> 32.4 us  [the longest x1 13.2 us: strided_attention(): q_heads = all_q.reshape(rows_all, cols_here, SH, HD)]
    all_to_all x7 -> x2, starting transfers between devices: 33.9 us -> 7.28 us  [the longest x1 3.65 us: strided_attention(): back = lax.all_to_all(mixed, 'seq', split_axis=0, concat_axis=1, tiled=True)]
    all_to_all x7 -> x1, local copies, waits for them, and re-layouts: 25.5 us -> 0.53 us  [strided_attention(): back = lax.all_to_all(mixed, 'seq', split_axis=0, concat_axis=1, tiled=True)]
    all_gather x0 -> x1, waiting for transfers between devices: none -> 23.7 us  [strided_attention(): all_q = lax.all_gather(plane_q, 'grp', axis=0, tiled=True)]
    all_to_all x0 -> x1, blocking collectives: none -> 20.8 us  [strided_attention(): lax.all_to_all(own_q, 'seq', split_axis=1, concat_axis=0, tiled=True)]
  transfers between devices with their start and end apart: 7 -> 5, of which waited for: 6 -> 4; matrix products, arithmetic and copies ran while one was open for 15% -> 25% of each run, Pallas kernels for 0% -> 0%
where the time goes in v1:
time: 467 us; the launch traced here: 458 us
  waiting for transfers between devices  174 us (37%)
  local copies, waits for them, and re-layouts  156 us (33%)
  matrix products  40.9 us (9%)
  other arithmetic  39.5 us (8%)
  blocking collectives  20.8 us (4%)
  between operations  13.5 us (3%)
  starting transfers between devices  7.36 us (2%)
  loops' own time  6.38 us (1%)
    reduce_scatter x1, waiting for transfers between devices, strided_attention(): summed = lax.psum_scatter(packed, 'grp', scatter_dimension=0, tiled=True)  138 us
    all_gather x1, waiting for transfers between devices, strided_attention(): all_q = lax.all_gather(plane_q, 'grp', axis=0, tiled=True)  23.7 us
    all_to_all x1, blocking collectives, strided_attention(): lax.all_to_all(own_q, 'seq', split_axis=1, concat_axis=0, tiled=True)  20.8 us
    unnamed x17, local copies, waits for them, and re-layouts  20.2 us
    concatenate x3, local copies, waits for them, and re-layouts, strided_attention(): k_here = jnp.concatenate([cache_kv[0], plane_kv[0]], axis=0)  19.6 us
    transpose x1, local copies, waits for them, and re-layouts, strided_attention(): jnp.einsum('chrm,mchd->rchd', expo.astype(jnp.bfloat16), v_heads, preferr...  19.3 us
    concatenate x3, local copies, waits for them, and re-layouts, strided_attention(): v_here = jnp.concatenate([cache_kv[1], plane_kv[1]], axis=0)  19.1 us
    slice x2, local copies, waits for them, and re-layouts, strided_attention(): v_here = jnp.concatenate([cache_kv[1], plane_kv[1]], axis=0)  18.4 us
  transfers between devices with their start and end apart: 5, of which 4 were waited for; matrix products, arithmetic and copies ran while one was open for 25% of the time, Pallas kernels for 0%

profile of v1, /device:TPU:0, one launch (start us, length us, event | category | flops | bytes accessed | tf_op | source)
XLA Modules:
  0.0 458.2 jit_solution(13270170238044575827)
XLA Ops:
  11.3 7.0 %reduce.4 = bf16[1024,512]{1,0:T(8,128)(2,1)S(1)} reduce(bf16[1024,1,512]{2,1,0:T(2,128)(2,1)S(1)} %bitcast.84, bf16[]{:T(256)} %broadcast.73), dimensions={1}, to_apply=%bitcast.63.reduce_sub_computation | reduce | bytes 2097154
  19.2 20.8 %all_to_all.30 = bf16[8,2,32768]{2,1,0:T(2,128)(2,1)S(1)} all-to-all(bf16[8,2,32768]{2,1,0:T(2,128)(2,1)S(1)} %reshape.122), channel_id=1, replica_groups=mesh['grp'=4,'seq'=8] {'seq'}, dimensions={0} | all-to-all | bytes 2097152 | tf_op jit(solution)/shard_map/all_to_all | solution.py:60
  42.3 3.8 fusion.49
  46.3 3.5 copy.73
  49.7 3.6 all-to-all-start
  53.4 6.0 %fusion.48 = (bf16[1,32,128,512]{3,2,1,0:T(8,128)(2,1)}, bf16[1,32,128,512]{3,2,1,0:T(8,128)(2,1)}) fusion(bf16[2,32,128,512]{3,2,1,0:T(8,128)(2,1)} %param.10), kind=kLoop, calls=%fused_computation.62 | loop fusion | bytes 16777216 | tf_op jit(solution)/shard_map/slice | solution.py:66
  59.4 6.4 %copy.97 = bf16[1,32,128,512]{2,3,1,0:T(8,128)(2,1)} copy(bf16[1,32,128,512]{3,2,1,0:T(8,128)(2,1)} %get-tuple-element.151) | data formatting | bytes 8388608
  65.8 13.1 %copy.79 = bf16[32,128,8,64]{3,0,2,1:T(8,128)(2,1)} copy(bf16[32,128,8,64]{1,3,2,0:T(8,128)(2,1)} %bitcast.79) | data formatting | bytes 8388608 | tf_op jit(solution)/shard_map/concatenate | solution.py:65
  79.9 12.4 %slice_reduce_fusion.1 = (bf16[1024,512]{1,0:T(8,128)(2,1)S(1)}, bf16[1024,512]{1,0:T(8,128)(2,1)}) fusion(bf16[2,1,1024,512]{3,0,1,2:T(2,128)(2,1)S(1)} %all-to-all-done), kind=kLoop, calls=%fused_computation.41 | loop fusion | bytes 4194304 | tf_op jit(solution)/shard_map/slice | solution.py:66
  95.1 3.8 copy.80
  98.9 23.7 %all-gather.2.cloned.1.call-done = bf16[32,128,512]{2,1,0:T(8,128)(2,1)} async-done(((bf16[8,128,512]{2,1,0:T(8,128)(2,1)}), bf16[32,128,512]{2,1,0:T(8,128)(2,1)}) %all-gather.2.cloned.1.call-update) | async-done | bytes 4194320 | tf_op jit(solution)/shard_map/all_gather | solution.py:63
  122.5 6.4 %copy.82 = bf16[32,128,512]{1,2,0:T(8,128)(2,1)} copy(bf16[32,128,512]{2,1,0:T(8,128)(2,1)} %all-gather.2.cloned.1.call-done) | data formatting | bytes 8388608 | tf_op jit(solution)/shard_map/all_gather | solution.py:63
  129.0 13.2 %copy.83 = bf16[32,128,8,64]{3,0,2,1:T(8,128)(2,1)} copy(bf16[32,128,8,64]{1,3,2,0:T(8,128)(2,1)} %bitcast.80) | data formatting | bytes 8388608 | tf_op jit(solution)/shard_map/reshape | solution.py:78
  142.2 13.5 %fusion.26 = (f32[128,8,32]{2,1,0:T(8,128)}, f32[128,8,40,32]{2,3,1,0:T(8,128)}) fusion(pred[32,40]{1,0:T(8,128)(4,1)S(1)} %compare_and_fusion, bf16[32,128,8,64]{3,0,2,1:T(8,128)(2,1)} %copy.83, bf16[8,128,8,64]{3,0,2,1:T(8,128)(2,1)S(1)} %copy-done.3, bf16[32,128,8,64]{3,0,2,1:T(8,128)(2,1)} %copy.79), kind=kOutput, calls=%fused_computation.25 | convolution fusion | flops 182157312 | bytes 14812416 | tf_op jit(solution)/shard_map/rchd,mchd->chrm/dot_general | solution.py:82
  155.8 6.5 %copy.96 = bf16[1,32,128,512]{2,3,1,0:T(8,128)(2,1)} copy(bf16[1,32,128,512]{3,2,1,0:T(8,128)(2,1)} %get-tuple-element.150) | data formatting | bytes 8388608
  162.3 13.1 %copy.75 = bf16[32,128,8,64]{3,0,2,1:T(8,128)(2,1)} copy(bf16[32,128,8,64]{1,3,2,0:T(8,128)(2,1)} %bitcast.81) | data formatting | bytes 8388608 | tf_op jit(solution)/shard_map/concatenate | solution.py:66
  177.4 4.0 copy.76
  181.4 11.6 %all-reduce.2.cloned.1.call-done = f32[128,8,32]{2,1,0:T(8,128)} async-done(((f32[128,8,32]{2,1,0:T(8,128)}), f32[128,8,32]{2,1,0:T(8,128)}) %all-reduce.2.cloned.1.call-update) | async-done | bytes 131088 | tf_op jit(solution)/shard_map/pmax | solution.py:85
  193.0 12.2 %fusion.35 = f32[32,128,8,64]{3,0,2,1:T(8,128)S(1)} fusion(bf16[8,128,8,64]{3,0,2,1:T(8,128)(2,1)S(1)} %copy.76, bf16[32,128,8,64]{3,0,2,1:T(8,128)(2,1)} %copy.75, f32[128,8,40,32]{2,3,1,0:T(8,128)} %get-tuple-element.159, f32[128,8,32]{2,1,0:T(8,128)} %all-reduce.2.cloned.1.call-done, pred[32,40]{1,0:T(8,128)(4,1)S(1)} %compare_and_fusion), kind=kOutput, calls=%fused_computation.35 | convolution fusion | flops 183500800 | bytes 19006720 | tf_op jit(solution)/shard_map/chrm,mchd->rchd/dot_general | solution.py:88
  205.2 19.3 %copy.84 = f32[32,128,8,64]{3,2,1,0:T(8,128)} copy(f32[32,128,8,64]{3,0,2,1:T(8,128)S(1)} %fusion.35) | data formatting | bytes 16777216 | tf_op jit(solution)/shard_map/chrm,mchd->rchd/transpose | solution.py:88
  224.5 10.9 %reshape.113 = f32[32,65536]{1,0:T(8,128)} reshape(f32[32,128,8,64]{3,2,1,0:T(8,128)} %copy.84) | data formatting | bytes 16777216 | tf_op jit(solution)/shard_map/reshape | solution.py:93
  235.5 11.4 %fusion.24 = f32[128,8,32]{2,1,0:T(8,128)S(1)} fusion(f32[128,8,40,32]{2,3,1,0:T(8,128)} %get-tuple-element.159, f32[128,8,32]{2,1,0:T(8,128)S(1)} %copy-done.2, pred[32,40]{1,0:T(8,128)(4,1)S(1)} %compare_and_fusion), kind=kLoop, calls=%fused_computation.23 | loop fusion | flops 5210112 | bytes 5506304 | tf_op jit(solution)/shard_map/reduce_sum | solution.py:87
  247.0 7.2 %pad_maximum_fusion = f32[32,66560]{1,0:T(8,128)} fusion(f32[32,1024]{1,0:T(8,128)S(1)} %copy.85, f32[32,65536]{1,0:T(8,128)} %reshape.113), kind=kLoop, calls=%fused_computation.34 | loop fusion | flops 2129920 | bytes 17039360 | tf_op jit(solution)/shard_map/concatenate | solution.py:91
  263.0 137.9 %reduce-scatter.2.cloned.1.call-done = f32[8,66560]{1,0:T(8,128)} async-done(((f32[32,66560]{1,0:T(8,128)}), f32[8,66560]{1,0:T(8,128)}) %reduce-scatter.2.cloned.1.call-update) | async-done | bytes 2129936 | tf_op jit(solution)/shard_map/reduce_scatter | solution.py:98
  400.9 3.1 slice.53
  403.9 3.0 copy.87
  410.1 3.6 all-to-all-start.2
  413.8 34.0 %while.13 = (s32[]{:T(128)}, bf16[2,512,512]{1,2,0:T(8,128)(2,1)}, s32[2]{0:T(128)S(1)}, bf16[2,512,8,64]{1,3,2,0:T(8,128)(2,1)S(1)}, bf16[1,1024,8,64]{1,3,2,0:...) while((s32[]{:T(128)}, bf16[2,512,512]{1,2,0:T(8,128)(2,1)}, ...), condition=%wide.region_3.4_spmd.clone, body=%wide.region_0.3_spmd.clone.sunk | while | flops 1120920064 | bytes 69292392 | solution.py:43
  420.8 4.2 fusion.61
  425.0 4.7 %fusion.62 = bf16[512,8,64]{0,2,1:T(8,128)(2,1)S(1)} fusion(bf16[1,1024,8,64]{1,3,2,0:T(8,128)(2,1)S(1)} %copy-done.4, f32[8,512,1024]{2,1,0:T(8,128)S(1)} %get-tuple-element.203, f32[8,512]{1,0:T(8,128)S(1)} %get-tuple-element.204, pred[512,1024]{1,0:T(8,128)(4,1)S(1)} %iota_compare_fusion.2, f32[512,8]{0,1:T(8,128)S(1)} %bitcast.91), kind=kOutput, calls=%fused_computation.13.clone.1 | convolution fusion | flops 554172416 | bytes 18907136 | tf_op jit(solution)/shard_map/while/body/eval_jaxpr/hqk,khd->qhd/dot_general | solution.py:38
  437.8 4.2 fusion.61
  442.0 4.7 %fusion.62 = bf16[512,8,64]{0,2,1:T(8,128)(2,1)S(1)} fusion(bf16[1,1024,8,64]{1,3,2,0:T(8,128)(2,1)S(1)} %copy-done.4, f32[8,512,1024]{2,1,0:T(8,128)S(1)} %get-tuple-element.203, f32[8,512]{1,0:T(8,128)S(1)} %get-tuple-element.204, pred[512,1024]{1,0:T(8,128)(4,1)S(1)} %iota_compare_fusion.2, f32[512,8]{0,1:T(8,128)S(1)} %bitcast.91), kind=kOutput, calls=%fused_computation.13.clone.1 | convolution fusion | flops 554172416 | bytes 18907136 | tf_op jit(solution)/shard_map/while/body/eval_jaxpr/hqk,khd->qhd/dot_general | solution.py:38
  (69 shorter events, 39.6 us)
Async XLA Ops:
  6.5 116.0 %all-gather.2.cloned.1.call-start = ((), (), s32[]{:S(2)}) async-start(), calls=%async_computation.4 | async-start | bytes 5242880 | tf_op jit(solution)/shard_map/all_gather | solution.py:63
  49.7 30.2 %all-to-all-start = ((bf16[2,1,1024,512]{3,0,1,2:T(2,128)(2,1)}), bf16[2,1,1024,512]{3,0,1,2:T(2,128)(2,1)S(1)}, u32[]{:S(2)}, u32[]{:S(2)}) async-start(bf16[2,1,1024,512]{3,0,1,2:T(2,128)(2,1)} %copy.73), calls=%async_computation | async-start | bytes 4194304 | tf_op jit(solution)/shard_map/all_to_all | solution.py:61
  53.4 139.7 %all-reduce.2.cloned.1.call-start = ((), (), s32[]{:S(2)}) async-start(), calls=%async_computation.5 | async-start | bytes 1048576 | tf_op jit(solution)/shard_map/pmax | solution.py:85
  65.8 13.2 %copy-start.7 = (s32[32]{0:T(128)S(1)}, s32[32]{0:T(128)}, u32[]{:S(2)}) copy-start(s32[32]{0:T(128)} %param.11) | copy-start | bytes 388
  129.0 13.2 %copy-start.3 = (bf16[8,128,8,64]{3,0,2,1:T(8,128)(2,1)S(1)}, bf16[8,128,8,64]{3,0,2,1:T(8,128)(2,1)}, u32[]{:S(2)}) copy-start(bf16[8,128,8,64]{3,0,2,1:T(8,128)(2,1)} %copy.80) | copy-start | bytes 3145732
  155.7 245.2 %reduce-scatter.2.cloned.1.call-start = ((), (), s32[]{:S(2)}) async-start(), calls=%async_computation.6 | async-start | bytes 10649600 | tf_op jit(solution)/shard_map/reduce_scatter | solution.py:98
  224.5 10.9 %copy-start.2 = (f32[128,8,32]{2,1,0:T(8,128)S(1)}, f32[128,8,32]{2,1,0:T(8,128)}, u32[]{:S(2)}) copy-start(f32[128,8,32]{2,1,0:T(8,128)} %all-reduce.2.cloned.1.call-done) | copy-start | bytes 393220
  254.2 1.2 copy-start
  254.2 8.3 %copy-start.1 = (bf16[1024,512]{1,0:T(8,128)(2,1)S(1)}, bf16[1024,512]{1,0:T(8,128)(2,1)}, u32[]{:S(2)}) copy-start(bf16[1024,512]{1,0:T(8,128)(2,1)} %get-tuple-element.163) | copy-start | bytes 3145732
  400.9 6.0 %slice-start = ((f32[8,66560]{1,0:T(8,128)}), f32[8,1024]{1,0:T(8,128)S(1)}, s32[]{:S(2)}) async-start(f32[8,66560]{1,0:T(8,128)} %reduce-scatter.2.cloned.1.call-done), calls=%async_computation.7 | async-start | bytes 65536 | tf_op jit(solution)/shard_map/slice | solution.py:100
  410.1 39.2 %all-to-all-start.2 = ((bf16[8,128,512]{1,2,0:T(8,128)(2,1)}), bf16[8,128,512]{1,2,0:T(8,128)(2,1)S(1)}, u32[]{:S(2)}, u32[]{:S(2)}) async-start(bf16[8,128,512]{1,2,0:T(8,128)(2,1)} %fusion.43), calls=%async_computation.3 | async-start | bytes 2097152 | tf_op jit(solution)/shard_map/all_to_all | solution.py:103
  420.8 4.2 copy-start.4
  425.0 4.7 %copy-start.5 = (bf16[2,512,512]{1,2,0:T(8,128)(2,1)S(1)}, bf16[2,512,512]{1,2,0:T(8,128)(2,1)}, u32[]{:S(2)}) copy-start(bf16[2,512,512]{1,2,0:T(8,128)(2,1)} %get-tuple-element.216) | copy-start | bytes 3145732 | tf_op jit(solution)/shard_map/while
  429.8 1.0 copy-start.6
  437.8 4.2 copy-start.4
  442.0 4.7 %copy-start.5 = (bf16[2,512,512]{1,2,0:T(8,128)(2,1)S(1)}, bf16[2,512,512]{1,2,0:T(8,128)(2,1)}, u32[]{:S(2)}) copy-start(bf16[2,512,512]{1,2,0:T(8,128)(2,1)} %get-tuple-element.216) | copy-start | bytes 3145732 | tf_op jit(solution)/shard_map/while
  446.8 1.0 copy-start.6
Sparse Core Ops, SparseCore 0:
  42.4 80.0 all-gather.1
  155.8 37.1 all-reduce.1
  254.3 146.4 reduce-scatter.1

commit v2 on v1

--- a/solution.py
+++ b/solution.py
@@ -44,19 +44,16 @@
     return result.reshape(tok, LH * HD)
 
 
-def strided_attention(queries, keys, values, cache_kv, thread_start):
+def strided_attention(own_q, own_k, own_v, cache_kv, thread_start):
     scale = HD ** (-0.5)
-    width_l = LH * HD
     width_s = SH * HD
-    tok = queries.shape[0]
-    rows_dev = tok // STRIDE
+    rows_dev = own_q.shape[0]
     cache_here = cache_kv.shape[1]
     cols_here = cache_kv.shape[2]
     rows_all = thread_start.shape[0]
     grp = lax.axis_index("grp")
 
-    own_q = queries[:, width_l:].reshape(rows_dev, STRIDE, width_s)
-    own_kv = jnp.stack([keys[:, width_l:], values[:, width_l:]]).reshape(2, rows_dev, STRIDE, width_s)
+    own_kv = jnp.stack([own_k, own_v])
     plane_q = lax.all_to_all(own_q, "seq", split_axis=1, concat_axis=0, tiled=True)
     plane_kv = lax.all_to_all(own_kv, "seq", split_axis=2, concat_axis=1, tiled=True)
     rows_plane = plane_q.shape[0]
@@ -100,13 +97,37 @@
     total_mine = summed[:, cols_here * width_s :].reshape(rows_plane, cols_here, SH)
     mixed = (acc_mine / total_mine[..., None]).astype(jnp.bfloat16)
     mixed = mixed.reshape(rows_plane, cols_here, width_s)
-    back = lax.all_to_all(mixed, "seq", split_axis=0, concat_axis=1, tiled=True)
-    return back.reshape(tok, width_s)
+    return lax.all_to_all(mixed, "seq", split_axis=0, concat_axis=1, tiled=True)
+
+
+CHUNKS = 2
 
 
 def shards(queries, keys, values, cache_kv, thread_start):
     width_l = LH * HD
-    strided_out = strided_attention(queries, keys, values, cache_kv, thread_start)
+    width_s = SH * HD
+    cols_here = cache_kv.shape[2]
+    chunks = CHUNKS if cols_here % (CHUNKS * 16) == 0 else 1
+    step = cols_here // chunks
+    cols_dev = STRIDE // cols_here
+    q_cols = queries[:, width_l:].reshape(-1, cols_dev, cols_here, width_s)
+    k_cols = keys[:, width_l:].reshape(-1, cols_dev, cols_here, width_s)
+    v_cols = values[:, width_l:].reshape(-1, cols_dev, cols_here, width_s)
+    pieces = []
+    for part in range(chunks):
+        cut = slice(part * step, (part + 1) * step)
+        pieces.append(
+            strided_attention(
+                q_cols[:, :, cut].reshape(-1, cols_dev * step, width_s),
+                k_cols[:, :, cut].reshape(-1, cols_dev * step, width_s),
+                v_cols[:, :, cut].reshape(-1, cols_dev * step, width_s),
+                cache_kv[:, :, cut],
+                thread_start,
+            )
+        )
+    strided_out = jnp.concatenate(
+        [p.reshape(-1, cols_dev, step, width_s) for p in pieces], axis=2
+    ).reshape(-1, width_s)
     local_out = local_attention(queries[:, :width_l], keys[:, :width_l], values[:, :width_l])
     return jnp.concatenate([local_out.astype(jnp.bfloat16), strided_out], axis=1)
 

time: 467 us -> 485 us (1.039)
  waiting for transfers between devices: 174 us -> 149 us
  local copies, waits for them, and re-layouts: 156 us -> 173 us
  matrix products: 40.9 us -> 57.4 us
  starting transfers between devices: 7.36 us -> 20.3 us
  blocking collectives: 20.8 us -> 14.7 us
    reduce_scatter x1 -> x2, waiting for transfers between devices: 138 us -> 110 us  [strided_attention(): summed = lax.psum_scatter(packed, 'grp', scatter_dimension=0, tiled=True)]
    all_gather x1 -> x2, waiting for transfers between devices: 23.7 us -> 0.02 us  [strided_attention(): all_q = lax.all_gather(plane_q, 'grp', axis=0, tiled=True)]
    pmax x1 -> x2, waiting for transfers between devices: 11.6 us -> 34.9 us  [strided_attention(): top = lax.pmax(jnp.max(scores, axis=-1), 'grp')]
    concatenate x3 -> x8, local copies, waits for them, and re-layouts: 19.6 us -> 37.4 us  [strided_attention(): k_here = jnp.concatenate([cache_kv[0], plane_kv[0]], axis=0)]
    dot_general x1 -> x2, matrix products: 13.5 us -> 28.5 us  [strided_attention(): jnp.einsum('rchd,mchd->chrm', q_heads, k_heads, preferred_element_type=jn...]
    unnamed x17 -> x26, local copies, waits for them, and re-layouts: 20.2 us -> 9.18 us
    concatenate x3 -> x8, local copies, waits for them, and re-layouts: 19.1 us -> 29 us  [strided_attention(): v_here = jnp.concatenate([cache_kv[1], plane_kv[1]], axis=0)]
    all_to_all x1 -> x3, starting transfers between devices: 3.65 us -> 12.2 us  [the longest x2 8.08 us: strided_attention(): return lax.all_to_all(mixed, 'seq', split_axis=0, concat_axis=1, tiled=True)]
  transfers between devices with their start and end apart: 5 -> 11, of which waited for: 4 -> 5; matrix products, arithmetic and copies ran while one was open for 25% -> 46% of each run, Pallas kernels for 0% -> 0%
where the time goes in v2:
time: 485 us; the launch traced here: 476 us
  local copies, waits for them, and re-layouts  173 us (36%)
  waiting for transfers between devices  149 us (31%)
  matrix products  57.4 us (12%)
  other arithmetic  39.8 us (8%)
  starting transfers between devices  20.3 us (4%)
  blocking collectives  14.7 us (3%)
  between operations  14.3 us (3%)
  loops' own time  6.87 us (1%)
    reduce_scatter x2, waiting for transfers between devices, strided_attention(): summed = lax.psum_scatter(packed, 'grp', scatter_dimension=0, tiled=True)  110 us
    concatenate x8, local copies, waits for them, and re-layouts, strided_attention(): k_here = jnp.concatenate([cache_kv[0], plane_kv[0]], axis=0)  37.4 us
    pmax x2, waiting for transfers between devices, strided_attention(): top = lax.pmax(jnp.max(scores, axis=-1), 'grp')  34.9 us
    concatenate x8, local copies, waits for them, and re-layouts, strided_attention(): v_here = jnp.concatenate([cache_kv[1], plane_kv[1]], axis=0)  29 us
    dot_general x2, matrix products, strided_attention(): jnp.einsum('rchd,mchd->chrm', q_heads, k_heads, preferred_element_type=jn...  28.5 us
    slice x3, local copies, waits for them, and re-layouts, strided_attention(): v_here = jnp.concatenate([cache_kv[1], plane_kv[1]], axis=0)  18.4 us
    transpose x2, local copies, waits for them, and re-layouts, strided_attention(): jnp.einsum('chrm,mchd->rchd', expo.astype(jnp.bfloat16), v_heads, preferr...  16.1 us
    all_to_all x1, blocking collectives, strided_attention(): lax.all_to_all(own_q, 'seq', split_axis=1, concat_axis=0, tiled=True)  14.7 us
  transfers between devices with their start and end apart: 11, of which 5 were waited for; matrix products, arithmetic and copies ran while one was open for 46% of the time, Pallas kernels for 0%

profile of v2, /device:TPU:0, one launch (start us, length us, event | category | flops | bytes accessed | tf_op | source)
XLA Modules:
  0.0 475.6 jit_solution(7228319810027495082)
XLA Ops:
  14.8 14.7 %all_to_all.60 = bf16[8,2,16384]{2,1,0:T(2,128)(2,1)S(1)} all-to-all(bf16[8,2,16384]{2,1,0:T(2,128)(2,1)S(1)} %reshape.191), channel_id=1, replica_groups=mesh['grp'=4,'seq'=8] {'seq'}, dimensions={0} | all-to-all | bytes 1048576 | tf_op jit(solution)/shard_map/all_to_all | solution.py:57
  61.5 5.8 %fusion.78 = (bf16[1,32,64,512]{3,2,1,0:T(8,128)(2,1)S(1)}, bf16[1,32,64,512]{3,2,1,0:T(8,128)(2,1)}, bf16[1,32,64,512]{3,2,1,0:T(8,128)(2,1)}, bf16[1,32,64,512]{3,2,1,0:T(8,128)(2,1)}) fusion(bf16[2,32,128,512]{3,2,1,0:T(8,128)(2,1)} %param.10), kind=kLoop, calls=%fused_computation.90 | loop fusion | bytes 16777216 | tf_op jit(solution)/shard_map/slice | solution.py:63
  67.2 6.2 %concatenate.52 = bf16[32,64,8,64]{3,2,1,0:T(8,128)(2,1)} reshape(bf16[1,32,64,512]{3,2,1,0:T(8,128)(2,1)} %get-tuple-element.155) | data formatting | bytes 4194304 | tf_op jit(solution)/shard_map/concatenate | solution.py:62
  73.4 9.1 %copy.85 = bf16[32,64,8,64]{3,0,2,1:T(8,128)(2,1)} copy(bf16[32,64,8,64]{3,2,1,0:T(8,128)(2,1)} %concatenate.52) | data formatting | bytes 4194304 | tf_op jit(solution)/shard_map/concatenate | solution.py:62
  84.7 6.6 %concatenate.59 = bf16[32,64,8,64]{3,2,1,0:T(8,128)(2,1)} reshape(bf16[1,32,64,512]{3,2,1,0:T(8,128)(2,1)} %get-tuple-element.156) | data formatting | bytes 4194304 | tf_op jit(solution)/shard_map/concatenate | solution.py:62
  91.3 9.0 %copy.95 = bf16[32,64,8,64]{3,0,2,1:T(8,128)(2,1)} copy(bf16[32,64,8,64]{3,2,1,0:T(8,128)(2,1)} %concatenate.59) | data formatting | bytes 4194304 | tf_op jit(solution)/shard_map/concatenate | solution.py:62
  104.0 9.0 %copy.83 = bf16[32,64,8,64]{3,0,2,1:T(8,128)(2,1)} copy(bf16[32,64,8,64]{3,2,1,0:T(8,128)(2,1)} %concatenate.48) | data formatting | bytes 4194304 | tf_op jit(solution)/shard_map/concatenate | solution.py:63
  117.4 5.9 %slice_reduce_fusion.3 = (bf16[512,512]{1,0:T(8,128)(2,1)S(1)}, bf16[512,512]{1,0:T(8,128)(2,1)S(1)}) fusion(bf16[2,1,512,512]{3,0,1,2:T(2,128)(2,1)S(1)} %all-to-all-done), kind=kLoop, calls=%fused_computation.65 | loop fusion | bytes 2097152 | tf_op jit(solution)/shard_map/slice | solution.py:63
  126.0 6.3 %reshape.172 = bf16[32,64,8,64]{3,2,1,0:T(8,128)(2,1)} reshape(bf16[32,64,512]{2,1,0:T(8,128)(2,1)} %all-gather.3.cloned.1.call-done) | data formatting | bytes 4194304 | tf_op jit(solution)/shard_map/reshape | solution.py:75
  132.3 11.7 %fusion.28 = (f32[64,8,32]{2,1,0:T(8,128)}, f32[64,8,40,32]{2,3,1,0:T(8,128)}) fusion(pred[32,40]{1,0:T(8,128)(4,1)S(1)} %compare_and_fusion, bf16[32,64,8,64]{3,2,1,0:T(8,128)(2,1)} %reshape.172, bf16[8,64,8,64]{3,0,2,1:T(8,128)(2,1)S(1)} %copy-done.7, bf16[32,64,8,64]{3,0,2,1:T(8,128)(2,1)} %copy.85), kind=kOutput, calls=%fused_computation.29 | convolution fusion | flops 91078656 | bytes 7406848 | tf_op jit(solution)/shard_map/rchd,mchd->chrm/dot_general | solution.py:79
  144.1 6.7 %slice_reduce_fusion.1 = (bf16[512,512]{1,0:T(8,128)(2,1)S(1)}, bf16[512,512]{1,0:T(8,128)(2,1)}) fusion(bf16[2,1,512,512]{3,0,1,2:T(2,128)(2,1)S(1)} %all-to-all-done.3), kind=kLoop, calls=%fused_computation.63 | loop fusion | bytes 2097152 | tf_op jit(solution)/shard_map/slice | solution.py:63
  156.4 6.3 %reshape.178 = bf16[32,64,8,64]{3,2,1,0:T(8,128)(2,1)} reshape(bf16[32,64,512]{2,1,0:T(8,128)(2,1)} %all-gather.5.cloned.1.call-done) | data formatting | bytes 4194304 | tf_op jit(solution)/shard_map/reshape | solution.py:75
  162.7 18.6 %all-reduce.3.cloned.1.call-done = f32[64,8,32]{2,1,0:T(8,128)} async-done(((f32[64,8,32]{2,1,0:T(8,128)}), f32[64,8,32]{2,1,0:T(8,128)}) %all-reduce.3.cloned.1.call-update) | async-done | bytes 65552 | tf_op jit(solution)/shard_map/pmax | solution.py:82
  181.4 16.8 %fusion.24 = (f32[64,8,32]{2,1,0:T(8,128)S(1)}, f32[64,8,32]{2,1,0:T(8,128)}, f32[64,8,40,32]{2,3,1,0:T(8,128)}) fusion(f32[64,8,40,32]{2,3,1,0:T(8,128)} %get-tuple-element.171, f32[64,8,32]{2,1,0:T(8,128)} %all-reduce.3.cloned.1.call-done, pred[32,40]{1,0:T(8,128)(4,1)S(1)} %compare_and_fusion, bf16[32,64,8,64]{3,2,1,0:T(8,128)(2,1)} %reshape.178, ...), kind=kOutput, calls=%fused_computation.25 | convolution fusion | flops 93683712 | bytes 10159360 | tf_op jit(solution)/shard_map/rchd,mchd->chrm/dot_general | solution.py:79
  198.3 6.9 %fusion.63 = f32[32,64,8,64]{3,0,2,1:T(8,128)S(1)} fusion(f32[64,8,40,32]{2,3,1,0:T(8,128)} %get-tuple-element.171, f32[64,8,32]{2,1,0:T(8,128)S(1)} %copy-done.8, pred[32,40]{1,0:T(8,128)(4,1)S(1)} %compare_and_fusion, bf16[8,64,8,64]{3,0,2,1:T(8,128)(2,1)S(1)} %copy.84, bf16[32,64,8,64]{3,0,2,1:T(8,128)(2,1)} %copy.83), kind=kOutput, calls=%fused_computation.60 | convolution fusion | flops 91750400 | bytes 9504000 | tf_op jit(solution)/shard_map/chrm,mchd->rchd/dot_general | solution.py:85
  205.2 8.1 %copy.89 = f32[32,64,8,64]{3,2,1,0:T(8,128)} copy(f32[32,64,8,64]{3,0,2,1:T(8,128)S(1)} %fusion.63) | data formatting | bytes 8388608 | tf_op jit(solution)/shard_map/chrm,mchd->rchd/transpose | solution.py:85
  213.3 6.9 %reshape.173 = f32[32,32768]{1,0:T(8,128)} reshape(f32[32,64,8,64]{3,2,1,0:T(8,128)} %copy.89) | data formatting | bytes 8388608 | tf_op jit(solution)/shard_map/reshape | solution.py:90
  220.3 4.6 pad_maximum_fusion
  228.8 9.0 %copy.93 = bf16[32,64,8,64]{3,0,2,1:T(8,128)(2,1)} copy(bf16[32,64,8,64]{3,2,1,0:T(8,128)(2,1)} %concatenate.56) | data formatting | bytes 4194304 | tf_op jit(solution)/shard_map/concatenate | solution.py:63
  239.5 16.3 %all-reduce.5.cloned.1.call-done = f32[64,8,32]{2,1,0:T(8,128)} async-done(((f32[64,8,32]{2,1,0:T(8,128)}), f32[64,8,32]{2,1,0:T(8,128)}) %all-reduce.5.cloned.1.call-update) | async-done | bytes 65552 | tf_op jit(solution)/shard_map/pmax | solution.py:82
  255.8 6.7 %fusion.58 = f32[32,64,8,64]{3,0,2,1:T(8,128)S(1)} fusion(f32[64,8,40,32]{2,3,1,0:T(8,128)} %get-tuple-element.172, f32[64,8,32]{2,1,0:T(8,128)} %all-reduce.5.cloned.1.call-done, pred[32,40]{1,0:T(8,128)(4,1)S(1)} %compare_and_fusion, bf16[8,64,8,64]{3,0,2,1:T(8,128)(2,1)S(1)} %copy.94, bf16[32,64,8,64]{3,0,2,1:T(8,128)(2,1)} %copy.93), kind=kOutput, calls=%fused_computation.59 | convolution fusion | flops 91750400 | bytes 9504000 | tf_op jit(solution)/shard_map/chrm,mchd->rchd/dot_general | solution.py:85
  262.5 8.1 %copy.99 = f32[32,64,8,64]{3,2,1,0:T(8,128)} copy(f32[32,64,8,64]{3,0,2,1:T(8,128)S(1)} %fusion.58) | data formatting | bytes 8388608 | tf_op jit(solution)/shard_map/chrm,mchd->rchd/transpose | solution.py:85
  270.6 7.0 %reshape.179 = f32[32,32768]{1,0:T(8,128)} reshape(f32[32,64,8,64]{3,2,1,0:T(8,128)} %copy.99) | data formatting | bytes 8388608 | tf_op jit(solution)/shard_map/reshape | solution.py:90
  277.6 6.9 %fusion.26 = f32[64,8,32]{2,1,0:T(8,128)S(1)} fusion(f32[64,8,40,32]{2,3,1,0:T(8,128)} %get-tuple-element.172, f32[64,8,32]{2,1,0:T(8,128)S(1)} %copy-done.4, pred[32,40]{1,0:T(8,128)(4,1)S(1)} %compare_and_fusion), kind=kLoop, calls=%fused_computation.27 | loop fusion | flops 2605056 | bytes 2753792 | tf_op jit(solution)/shard_map/reduce_sum | solution.py:84
  284.5 4.5 pad_maximum_fusion.1
  289.0 46.7 %reduce-scatter.3.cloned.1.call-done = f32[8,33280]{1,0:T(8,128)} async-done(((f32[32,33280]{1,0:T(8,128)}), f32[8,33280]{1,0:T(8,128)}) %reduce-scatter.3.cloned.1.call-update) | async-done | bytes 1064976 | tf_op jit(solution)/shard_map/reduce_scatter | solution.py:95
  352.8 63.5 %reduce-scatter.5.cloned.1.call-done = f32[8,33280]{1,0:T(8,128)} async-done(((f32[32,33280]{1,0:T(8,128)}), f32[8,33280]{1,0:T(8,128)}) %reduce-scatter.5.cloned.1.call-update) | async-done | bytes 1064976 | tf_op jit(solution)/shard_map/reduce_scatter | solution.py:95
  429.8 34.2 %while.13 = (s32[]{:T(128)}, bf16[2,512,512]{1,2,0:T(8,128)(2,1)}, s32[2]{0:T(128)S(1)}, bf16[2,512,8,64]{1,3,2,0:T(8,128)(2,1)S(1)}, bf16[1,1024,8,64]{1,3,2,0:...) while((s32[]{:T(128)}, bf16[2,512,512]{1,2,0:T(8,128)(2,1)}, ...), condition=%wide.region_3.4_spmd.clone, body=%wide.region_0.3_spmd.clone.sunk | while | flops 1120920064 | bytes 60904232 | solution.py:43
  437.2 4.2 fusion.93
  441.4 4.7 fusion.94
  454.3 4.2 fusion.93
  458.5 4.7 fusion.94
  (115 shorter events, 108.9 us)
Async XLA Ops:
  6.5 119.5 %all-gather.3.cloned.1.call-start = ((), (), s32[]{:S(2)}) async-start(), calls=%async_computation.8 | async-start | bytes 2621440 | tf_op jit(solution)/shard_map/all_gather | solution.py:60
  36.8 13.9 %all-to-all-start.4 = ((bf16[8,2,16384]{2,1,0:T(2,128)(2,1)}), bf16[8,2,16384]{2,1,0:T(2,128)(2,1)}, u32[]{:S(2)}, u32[]{:S(2)}) async-start(bf16[8,2,16384]{2,1,0:T(2,128)(2,1)} %reshape.189), calls=%async_computation.5 | async-start | bytes 1048576 | tf_op jit(solution)/shard_map/all_to_all | solution.py:57
  41.0 115.5 %all-gather.5.cloned.1.call-start = ((), (), s32[]{:S(2)}) async-start(), calls=%async_computation.11 | async-start | bytes 2621440 | tf_op jit(solution)/shard_map/all_gather | solution.py:60
  57.9 55.3 %all-to-all-start = ((bf16[2,1,512,512]{3,0,1,2:T(2,128)(2,1)}), bf16[2,1,512,512]{3,0,1,2:T(2,128)(2,1)S(1)}, u32[]{:S(2)}, u32[]{:S(2)}) async-start(bf16[2,1,512,512]{3,0,1,2:T(2,128)(2,1)} %copy.82), calls=%async_computation | async-start | bytes 2097152 | tf_op jit(solution)/shard_map/all_to_all | solution.py:58
  73.4 9.1 %copy-start.2 = (bf16[1,8,64,512]{3,2,1,0:T(8,128)(2,1)S(1)}, bf16[1,8,64,512]{3,2,1,0:T(8,128)(2,1)}, u32[]{:S(2)}) copy-start(bf16[1,8,64,512]{3,2,1,0:T(8,128)(2,1)} %get-tuple-element.167) | copy-start | bytes 1572868
  73.4 9.1 %copy-start.3 = (bf16[1,8,64,512]{3,2,1,0:T(8,128)(2,1)S(1)}, bf16[1,8,64,512]{3,2,1,0:T(8,128)(2,1)}, u32[]{:S(2)}) copy-start(bf16[1,8,64,512]{3,2,1,0:T(8,128)(2,1)} %get-tuple-element.169) | copy-start | bytes 1572868
  104.0 9.1 %copy-start.9 = (s32[32]{0:T(128)S(1)}, s32[32]{0:T(128)}, u32[]{:S(2)}) copy-start(s32[32]{0:T(128)} %param.11) | copy-start | bytes 388
  113.2 30.9 %all-to-all-start.3 = ((bf16[2,1,512,512]{3,0,1,2:T(2,128)(2,1)}), bf16[2,1,512,512]{3,0,1,2:T(2,128)(2,1)S(1)}, u32[]{:S(2)}, u32[]{:S(2)}) async-start(bf16[2,1,512,512]{3,0,1,2:T(2,128)(2,1)} %copy.92), calls=%async_computation.4 | async-start | bytes 2097152 | tf_op jit(solution)/shard_map/all_to_all | solution.py:58
  117.3 64.1 %all-reduce.3.cloned.1.call-start = ((), (), s32[]{:S(2)}) async-start(), calls=%async_computation.9 | async-start | bytes 524288 | tf_op jit(solution)/shard_map/pmax | solution.py:82
  126.0 6.3 %copy-start.7 = (bf16[8,64,8,64]{3,0,2,1:T(8,128)(2,1)S(1)}, bf16[8,64,8,64]{3,0,2,1:T(8,128)(2,1)}, u32[]{:S(2)}) copy-start(bf16[8,64,8,64]{3,0,2,1:T(8,128)(2,1)} %copy.86) | copy-start | bytes 1572868
  144.0 111.8 %all-reduce.5.cloned.1.call-start = ((), (), s32[]{:S(2)}) async-start(), calls=%async_computation.12 | async-start | bytes 524288 | tf_op jit(solution)/shard_map/pmax | solution.py:82
  156.4 25.0 %copy-start.6 = (bf16[8,64,8,64]{3,0,2,1:T(8,128)(2,1)S(1)}, bf16[8,64,8,64]{3,0,2,1:T(8,128)(2,1)}, u32[]{:S(2)}) copy-start(bf16[8,64,8,64]{3,0,2,1:T(8,128)(2,1)} %copy.96) | copy-start | bytes 1572868
  181.4 16.9 %copy-start.8 = (f32[64,8,32]{2,1,0:T(8,128)S(1)}, f32[64,8,32]{2,1,0:T(8,128)}, u32[]{:S(2)}) copy-start(f32[64,8,32]{2,1,0:T(8,128)} %all-reduce.3.cloned.1.call-done) | copy-start | bytes 196612
  220.2 4.7 copy-start
  220.2 115.5 %reduce-scatter.3.cloned.1.call-start = ((), (), s32[]{:S(2)}) async-start(), calls=%async_computation.10 | async-start | bytes 5324800 | tf_op jit(solution)/shard_map/reduce_scatter | solution.py:95
  224.9 191.4 %reduce-scatter.5.cloned.1.call-start = ((), (), s32[]{:S(2)}) async-start(), calls=%async_computation.13 | async-start | bytes 5324800 | tf_op jit(solution)/shard_map/reduce_scatter | solution.py:95
  270.6 7.0 %copy-start.4 = (f32[64,8,32]{2,1,0:T(8,128)S(1)}, f32[64,8,32]{2,1,0:T(8,128)}, u32[]{:S(2)}) copy-start(f32[64,8,32]{2,1,0:T(8,128)} %all-reduce.5.cloned.1.call-done) | copy-start | bytes 196612
  337.7 6.8 %copy-start.1 = (bf16[1024,512]{1,0:T(8,128)(2,1)S(1)}, bf16[1024,512]{1,0:T(8,128)(2,1)}, u32[]{:S(2)}) copy-start(bf16[1024,512]{1,0:T(8,128)(2,1)} %get-tuple-element.162) | copy-start | bytes 3145732
  340.5 85.2 %all-to-all-start.2 = ((bf16[8,64,512]{2,1,0:T(8,128)(2,1)}), bf16[8,64,512]{2,1,0:T(8,128)(2,1)S(1)}, u32[]{:S(2)}, u32[]{:S(2)}) async-start(bf16[8,64,512]{2,1,0:T(8,128)(2,1)} %fusion.69), calls=%async_computation.3 | async-start | bytes 1048576 | tf_op jit(solution)/shard_map/all_to_all | solution.py:100
  425.7 39.9 %all-to-all-start.5 = ((bf16[8,64,512]{2,1,0:T(8,128)(2,1)}), bf16[8,64,512]{2,1,0:T(8,128)(2,1)}, u32[]{:S(2)}, u32[]{:S(2)}) async-start(bf16[8,64,512]{2,1,0:T(8,128)(2,1)} %fusion.68), calls=%async_computation.7 | async-start | bytes 1048576 | tf_op jit(solution)/shard_map/all_to_all | solution.py:100
  437.2 4.2 copy-start.5
  454.3 4.2 copy-start.5
Sparse Core Ops, SparseCore 0:
  31.1 45.0 all-gather.2
  77.7 44.4 all-gather.4
  144.1 37.1 all-reduce.2
  220.3 35.3 all-reduce.4
  257.9 77.7 reduce-scatter.2
  337.8 78.3 reduce-scatter.4
